TPU v7x, 512 devices: a whole 4x8x8 slice. The times are simulated.
512 devices in a mesh: chan: 32 (over y_hi, x, core), tm: 16 (over y_lo, z).
Axes of the slice: x: 4, y: 8 (y_hi: 4, y_lo: 2; y = y_hi * 2 + y_lo), z: 8, core: 2. Of those that a mesh axis runs over, the one named last changes fastest.
Arguments:
- raw_strain: float32 [2048, 16384], P('chan', 'tm'), may hold values from -2000 to 2000
- fir_taps: float32 [64], replicated, may hold values from -0.75 to 0.75
- block_mask: int32 [32, 32], replicated, may hold values 0 or 1
Outputs:
- correlations: float32 [128, 2048, 2048], P('tm', 'chan')
All inputs are finite; a program needn't handle non-finite values.
Results may differ from a plain program's by a relative error of at most 0.0054.
Values may be sent and summed in bfloat16 or wider, within the bound.
No kernel may reach another device: no remote copies, remote signals or barrier semaphores. Data moves between devices by JAX's collectives and lax.ppermute only.
A program may use at most 64 MiB of HBM per device.

v0:
```python
import math

import jax
import jax.numpy as jnp
from jax import lax
from jax.sharding import PartitionSpec as P

DECIM = 8
TAPS = 64
LAGS = 128


def from_behind(value, axis, steps):
    count = lax.axis_size(axis)
    first, last = (max(0, -steps), min(count, count - steps))
    return lax.ppermute(value, axis, [(source, source + steps) for source in range(first, last)])


def decimate(raw_strain, fir_taps):
    time_span = raw_strain.shape[1]
    margin = TAPS - DECIM
    earlier = from_behind(raw_strain[:, time_span - margin :], "tm", 1)
    extended = jnp.concatenate([earlier, raw_strain], axis=1)
    outputs = time_span // DECIM
    tap_blocks = TAPS // DECIM
    frames = outputs + tap_blocks - 1
    tap_table = fir_taps[::-1].reshape(tap_blocks, DECIM)
    shape_three = (frames, outputs, tap_blocks)
    matches = lax.broadcasted_iota(jnp.int32, shape_three, 0) - lax.broadcasted_iota(
        jnp.int32, shape_three, 1
    ) == lax.broadcasted_iota(jnp.int32, shape_three, 2)
    one_hot = matches.astype(jnp.float32)
    filter_matrix = jnp.einsum("mtj,jr->mrt", one_hot, tap_table, precision=lax.Precision.HIGHEST)
    filter_matrix = filter_matrix.reshape(frames * DECIM, outputs)
    return jnp.dot(
        extended, filter_matrix, precision=lax.Precision.HIGHEST, preferred_element_type=jnp.float32
    )


def per_device(raw_strain, fir_taps, block_mask):
    channel_rows = raw_strain.shape[0]
    decimated = decimate(raw_strain, fir_taps)
    rounded = decimated.astype(jnp.bfloat16)
    time_span = rounded.shape[1]
    tm_parts = lax.axis_size("tm")
    samples = time_span * tm_parts
    gathered = lax.all_gather(rounded, "tm", axis=1, tiled=True)
    full_values = gathered.astype(jnp.float32)
    root_whole = jnp.sqrt(jnp.mean(full_values * full_values, axis=1, keepdims=True) + 1e-06)
    caches = (full_values / root_whole).astype(jnp.bfloat16)
    lag_count = LAGS // tm_parts
    tm_index = lax.axis_index("tm")
    lag_base = tm_index * lag_count
    anchor = jnp.zeros((), jnp.int32)
    initial = jnp.zeros(
        (lag_count, channel_rows, channel_rows * lax.axis_size("chan")), jnp.float32
    )
    shard_piece = lax.all_gather(caches, "chan", axis=0, tiled=True)
    first_index = jnp.int32(0)
    piece_width = shard_piece.shape[0]
    padded_piece = jnp.pad(shard_piece, ((0, 0), (0, LAGS)))

    def one_lag(lag_step, running):
        shifted = lax.dynamic_slice_in_dim(padded_piece, lag_base + lag_step, samples, 1)
        product = lax.dot_general(
            caches, shifted, (((1,), (1,)), ((), ())), preferred_element_type=jnp.float32
        )
        where_at = (lag_step, anchor, first_index)
        current = lax.dynamic_slice(running, where_at, (1, channel_rows, piece_width))
        return lax.dynamic_update_slice(running, current + product[None], where_at)

    correlated = lax.fori_loop(0, lag_count, one_lag, initial)
    mask_row = lax.dynamic_index_in_dim(block_mask, lax.axis_index("chan"), 0, keepdims=False)
    weights = jnp.repeat(mask_row, channel_rows).astype(jnp.float32) * (1.0 / math.sqrt(samples))
    return correlated * weights[None, None, :]


def solution(mesh):
    placed = (P("chan", "tm"), P(), P())
    return jax.shard_map(
        per_device, mesh=mesh, in_specs=placed, out_specs=P("tm", "chan", None), check_vma=False
    )
```

profile of v0, /device:TPU:17, one launch (start us, length us, event | category | flops | bytes accessed | tf_op | source)
XLA Modules:
  0.0 219.1 jit_solution(5011104009306333967)
XLA Ops:
  6.5 0.0 all-gather.2.cloned.1.call-start
  6.5 0.8 slice.3
  7.4 4.0 %collective-permute-start = (f32[64,56]{1,0:T(8,128)S(1)}, f32[64,56]{1,0:T(8,128)S(1)}, u32[]{:S(2)}, u32[]{:S(2)}) collective-permute-start(f32[64,56]{1,0:T(8,128)S(1)} %slice.3), channel_id=1, source_target_pairs={{0,1},{1,2},{2,3},{3,4},{4,5},{5,6},{6,7},{7,8},{8,9},{9,10},{10,1... | collective-permute-start | bytes 43016 | tf_op jit(solution)/shard_map/ppermute | solution.py:16
  11.4 0.7 rev.3
  12.1 0.1 reshape.27
  12.2 0.4 convolution_bitcast_fusion
  12.6 0.0 collective-permute-done
  12.7 1.5 convolution_convert_fusion
  14.1 33.4 %all_gather.6 = bf16[64,2048]{1,0:T(8,128)(2,1)S(1)} all-gather(bf16[64,128]{1,0:T(8,128)(2,1)S(1)} %convolution_convert_fusion), channel_id=1, replica_groups=mesh['chan'=32,'tm'=16] {'tm'}, dimensions={1}, use_global_device_ids=true | all-gather | bytes 278528 | tf_op jit(solution)/shard_map/all_gather | solution.py:47
  47.5 0.2 fusion.12
  47.7 0.8 fusion.13
  48.5 0.0 all-gather.2.cloned.1.call-update
  48.6 0.7 multiply_bitcast_fusion
  49.3 0.1 broadcast_in_dim.16
  49.3 0.1 mul.36
  49.4 86.4 %all-gather.2.cloned.1.call-done = bf16[2048,2048]{1,0:T(8,128)(2,1)} async-done(((bf16[64,2048]{1,0:T(8,128)(2,1)}), bf16[2048,2048]{1,0:T(8,128)(2,1)}) %all-gather.2.cloned.1.call-update) | async-done | bytes 8388624 | tf_op jit(solution)/shard_map/all_gather | solution.py:58
  135.8 7.8 %pad.4 = bf16[2048,2176]{1,0:T(8,128)(2,1)} pad(bf16[2048,2048]{1,0:T(8,128)(2,1)} %all-gather.2.cloned.1.call-done, bf16[]{:T(256)} %constant.53.clone.1), padding=0_0x0_128 | pad | bytes 17301506 | tf_op jit(solution)/shard_map/jit(_pad)/pad | solution.py:61
  143.6 0.0 copy-start
  143.6 2.5 %broadcast_in_dim.15 = f32[8,64,2048]{2,1,0:T(8,128)} broadcast(f32[]{:T(128)} %constant.48.clone.1), dimensions={} | broadcast | bytes 4194308 | tf_op jit(solution)/shard_map/broadcast_in_dim | solution.py:55
  146.1 0.0 copy-done
  146.1 61.2 %while.13 = (s32[]{:T(128)}, f32[8,64,2048]{2,1,0:T(8,128)}, s32[]{:T(128)}, bf16[2048,2176]{1,0:T(8,128)(2,1)}, bf16[64,2048]{1,0:T(8,128)(2,1)S(1)}, /*index=5*/s32[]{:T(128)}, s32[]{:T(128)}, s32[]{:T(128)}) while((s32[]{:T(128)}, f32[8,64,2048]{2,1,0:T(8,128)}, s32[]{:T(128)}, bf16[2048,2176]{1,0:T(8,128)(2,1)}, ...), condition=%wide.region_2.3_spmd, body=%wide.region_1.2_spmd.sunk | while | flops 537001984 | bytes 9699475 | solution.py:72
  146.1 7.7 %fusion.26 = f32[8,64,2048]{2,1,0:T(8,128)} fusion(f32[8,64,2048]{2,1,0:T(8,128)} %get-tuple-element.150, s32[]{:T(128)S(6)} %copy.10, bf16[64,2048]{1,0:T(8,128)(2,1)S(1)} %get-tuple-element.161, bf16[2048,2176]{1,0:T(8,128)(2,1)} %get-tuple-element.160, s32[]{:T(128)S(6)} %select_n.19), kind=kOutput, calls=%fused_computation.4.clone.1 | convolution fusion | flops 537001984 | bytes 9699336 | tf_op jit(solution)/shard_map/while/body/eval_jaxpr/dot_general | solution.py:65
  153.8 7.7 %fusion.26 = f32[8,64,2048]{2,1,0:T(8,128)} fusion(f32[8,64,2048]{2,1,0:T(8,128)} %get-tuple-element.150, s32[]{:T(128)S(6)} %copy.10, bf16[64,2048]{1,0:T(8,128)(2,1)S(1)} %get-tuple-element.161, bf16[2048,2176]{1,0:T(8,128)(2,1)} %get-tuple-element.160, s32[]{:T(128)S(6)} %select_n.19), kind=kOutput, calls=%fused_computation.4.clone.1 | convolution fusion | flops 537001984 | bytes 9699336 | tf_op jit(solution)/shard_map/while/body/eval_jaxpr/dot_general | solution.py:65
  161.4 7.7 %fusion.26 = f32[8,64,2048]{2,1,0:T(8,128)} fusion(f32[8,64,2048]{2,1,0:T(8,128)} %get-tuple-element.150, s32[]{:T(128)S(6)} %copy.10, bf16[64,2048]{1,0:T(8,128)(2,1)S(1)} %get-tuple-element.161, bf16[2048,2176]{1,0:T(8,128)(2,1)} %get-tuple-element.160, s32[]{:T(128)S(6)} %select_n.19), kind=kOutput, calls=%fused_computation.4.clone.1 | convolution fusion | flops 537001984 | bytes 9699336 | tf_op jit(solution)/shard_map/while/body/eval_jaxpr/dot_general | solution.py:65
  169.1 7.7 %fusion.26 = f32[8,64,2048]{2,1,0:T(8,128)} fusion(f32[8,64,2048]{2,1,0:T(8,128)} %get-tuple-element.150, s32[]{:T(128)S(6)} %copy.10, bf16[64,2048]{1,0:T(8,128)(2,1)S(1)} %get-tuple-element.161, bf16[2048,2176]{1,0:T(8,128)(2,1)} %get-tuple-element.160, s32[]{:T(128)S(6)} %select_n.19), kind=kOutput, calls=%fused_computation.4.clone.1 | convolution fusion | flops 537001984 | bytes 9699336 | tf_op jit(solution)/shard_map/while/body/eval_jaxpr/dot_general | solution.py:65
  176.8 7.7 %fusion.26 = f32[8,64,2048]{2,1,0:T(8,128)} fusion(f32[8,64,2048]{2,1,0:T(8,128)} %get-tuple-element.150, s32[]{:T(128)S(6)} %copy.10, bf16[64,2048]{1,0:T(8,128)(2,1)S(1)} %get-tuple-element.161, bf16[2048,2176]{1,0:T(8,128)(2,1)} %get-tuple-element.160, s32[]{:T(128)S(6)} %select_n.19), kind=kOutput, calls=%fused_computation.4.clone.1 | convolution fusion | flops 537001984 | bytes 9699336 | tf_op jit(solution)/shard_map/while/body/eval_jaxpr/dot_general | solution.py:65
  184.4 7.7 %fusion.26 = f32[8,64,2048]{2,1,0:T(8,128)} fusion(f32[8,64,2048]{2,1,0:T(8,128)} %get-tuple-element.150, s32[]{:T(128)S(6)} %copy.10, bf16[64,2048]{1,0:T(8,128)(2,1)S(1)} %get-tuple-element.161, bf16[2048,2176]{1,0:T(8,128)(2,1)} %get-tuple-element.160, s32[]{:T(128)S(6)} %select_n.19), kind=kOutput, calls=%fused_computation.4.clone.1 | convolution fusion | flops 537001984 | bytes 9699336 | tf_op jit(solution)/shard_map/while/body/eval_jaxpr/dot_general | solution.py:65
  192.1 7.7 %fusion.26 = f32[8,64,2048]{2,1,0:T(8,128)} fusion(f32[8,64,2048]{2,1,0:T(8,128)} %get-tuple-element.150, s32[]{:T(128)S(6)} %copy.10, bf16[64,2048]{1,0:T(8,128)(2,1)S(1)} %get-tuple-element.161, bf16[2048,2176]{1,0:T(8,128)(2,1)} %get-tuple-element.160, s32[]{:T(128)S(6)} %select_n.19), kind=kOutput, calls=%fused_computation.4.clone.1 | convolution fusion | flops 537001984 | bytes 9699336 | tf_op jit(solution)/shard_map/while/body/eval_jaxpr/dot_general | solution.py:65
  199.7 7.7 %fusion.26 = f32[8,64,2048]{2,1,0:T(8,128)} fusion(f32[8,64,2048]{2,1,0:T(8,128)} %get-tuple-element.150, s32[]{:T(128)S(6)} %copy.10, bf16[64,2048]{1,0:T(8,128)(2,1)S(1)} %get-tuple-element.161, bf16[2048,2176]{1,0:T(8,128)(2,1)} %get-tuple-element.160, s32[]{:T(128)S(6)} %select_n.19), kind=kOutput, calls=%fused_computation.4.clone.1 | convolution fusion | flops 537001984 | bytes 9699336 | tf_op jit(solution)/shard_map/while/body/eval_jaxpr/dot_general | solution.py:65
  207.4 4.9 %broadcast_multiply_fusion = f32[8,64,2048]{2,1,0:T(8,128)} fusion(f32[8,64,2048]{2,1,0:T(8,128)} %get-tuple-element.99, f32[2048]{0:T(1024)S(1)} %mul.36), kind=kLoop, calls=%fused_computation.7 | loop fusion | flops 1048576 | bytes 8396800 | tf_op jit(solution)/shard_map/mul | solution.py:75
  (1 shorter events, 0.0 us)
Async XLA Ops:
  6.5 129.2 %all-gather.2.cloned.1.call-start = ((), (), s32[]{:S(2)}) async-start(), calls=%async_computation | async-start | bytes 8650752 | tf_op jit(solution)/shard_map/all_gather | solution.py:58
  7.4 5.3 %collective-permute-start = (f32[64,56]{1,0:T(8,128)S(1)}, f32[64,56]{1,0:T(8,128)S(1)}, u32[]{:S(2)}, u32[]{:S(2)}) collective-permute-start(f32[64,56]{1,0:T(8,128)S(1)} %slice.3), channel_id=1, source_target_pairs={{0,1},{1,2},{2,3},{3,4},{4,5},{5,6},{6,7},{7,8},{8,9},{9,10},{10,1... | collective-permute-start | bytes 43016 | tf_op jit(solution)/shard_map/ppermute | solution.py:16
  143.6 2.5 %copy-start = (bf16[64,2048]{1,0:T(8,128)(2,1)S(1)}, bf16[64,2048]{1,0:T(8,128)(2,1)}, u32[]{:S(2)}) copy-start(bf16[64,2048]{1,0:T(8,128)(2,1)} %fusion.13) | copy-start | bytes 786436
Sparse Core Ops, SparseCore 0:
  48.7 87.0 all-gather.1
where the time goes:
time: 219 us
  waiting for transfers between devices  86.4 us (39%)
  matrix products  63.1 us (29%)
  blocking collectives  33.4 us (15%)
  between operations  13.4 us (6%)
  local copies, waits for them, and re-layouts  12.1 us (6%)
  other arithmetic  6.58 us (3%)
  starting transfers between devices  3.99 us (2%)
    all_gather x1, waiting for transfers between devices, per_device(): shard_piece = lax.all_gather(caches, 'chan', axis=0, tiled=True)  86.4 us
    dot_general x8, matrix products, one_lag(): lax.dot_general(caches, shifted, (((1,), (1,)), ((), ())), preferred_elem...  61.2 us
    all_gather x1, blocking collectives, per_device(): gathered = lax.all_gather(rounded, 'tm', axis=1, tiled=True)  33.4 us
    pad x1, local copies, waits for them, and re-layouts, per_device(): padded_piece = jnp.pad(shard_piece, ((0, 0), (0, LAGS)))  7.82 us
    mul x1, other arithmetic, per_device(): return correlated * weights[None, None, :]  4.89 us
  transfers between devices with their start and end apart: 2, of which 1 were waited for; matrix products, arithmetic and copies ran while one was open for 1% of the time, Pallas kernels for 0%

commit v1 on v0

v1 whole, which is shorter than its diff:
```python
import math

import jax
import jax.numpy as jnp
from jax import lax
from jax.sharding import PartitionSpec as P

DECIM = 8
TAPS = 64
LAGS = 128


def from_behind(value, axis, steps):
    count = lax.axis_size(axis)
    first, last = (max(0, -steps), min(count, count - steps))
    return lax.ppermute(value, axis, [(source, source + steps) for source in range(first, last)])


def decimate(raw_strain, fir_taps):
    time_span = raw_strain.shape[1]
    margin = TAPS - DECIM
    earlier = from_behind(raw_strain[:, time_span - margin :], "tm", 1)
    extended = jnp.concatenate([earlier, raw_strain], axis=1)
    outputs = time_span // DECIM
    tap_blocks = TAPS // DECIM
    frames = outputs + tap_blocks - 1
    tap_table = fir_taps[::-1].reshape(tap_blocks, DECIM)
    shape_three = (frames, outputs, tap_blocks)
    matches = lax.broadcasted_iota(jnp.int32, shape_three, 0) - lax.broadcasted_iota(
        jnp.int32, shape_three, 1
    ) == lax.broadcasted_iota(jnp.int32, shape_three, 2)
    one_hot = matches.astype(jnp.float32)
    filter_matrix = jnp.einsum("mtj,jr->mrt", one_hot, tap_table, precision=lax.Precision.HIGHEST)
    filter_matrix = filter_matrix.reshape(frames * DECIM, outputs)
    return jnp.dot(
        extended, filter_matrix, precision=lax.Precision.HIGHEST, preferred_element_type=jnp.float32
    )


def per_device(raw_strain, fir_taps, block_mask):
    channel_rows = raw_strain.shape[0]
    chan_parts = lax.axis_size("chan")
    tm_parts = lax.axis_size("tm")
    decimated = decimate(raw_strain, fir_taps)
    rounded = decimated.astype(jnp.bfloat16)
    local_span = rounded.shape[1]
    samples = local_span * tm_parts
    values = rounded.astype(jnp.float32)
    square_sum = lax.psum(jnp.sum(values * values, axis=1, keepdims=True), "tm")
    root = jnp.sqrt(square_sum / samples + 1e-06)
    piece = (values / root).astype(jnp.bfloat16)

    gathered = lax.all_gather(piece, ("chan", "tm"), axis=0, tiled=False)
    gathered = gathered.reshape(chan_parts, tm_parts, channel_rows, local_span)
    whole = gathered.transpose(0, 2, 1, 3).reshape(chan_parts * channel_rows, samples)

    chan_index = lax.axis_index("chan")
    lag_count = LAGS // tm_parts
    lag_base = lax.axis_index("tm") * lag_count
    own = lax.dynamic_slice_in_dim(whole, chan_index * channel_rows, channel_rows, 0)
    reach = LAGS + lag_count
    padded = jnp.pad(own, ((0, 0), (reach, 0)))
    shifted = [
        lax.dynamic_slice_in_dim(padded, reach - lag_base - step, samples, 1)
        for step in range(lag_count)
    ]
    stacked = jnp.concatenate(shifted, axis=0)
    product = lax.dot_general(
        stacked, whole, (((1,), (1,)), ((), ())), preferred_element_type=jnp.float32
    )
    mask_row = lax.dynamic_index_in_dim(block_mask, chan_index, 0, keepdims=False)
    weights = jnp.repeat(mask_row, channel_rows).astype(jnp.float32) * (1.0 / math.sqrt(samples))
    return (product * weights[None, :]).reshape(lag_count, channel_rows, chan_parts * channel_rows)


def solution(mesh):
    placed = (P("chan", "tm"), P(), P())
    return jax.shard_map(
        per_device, mesh=mesh, in_specs=placed, out_specs=P("tm", "chan", None), check_vma=False
    )
```

time: 219 us -> 1540 us (7.03)
  the two profiles are of different devices: /device:TPU:17 before, /device:TPU:27 now
where the time goes in v1:
time: 1540 us
  waiting for transfers between devices  1450 us (94%)
  local copies, waits for them, and re-layouts  37.9 us (2%)
  blocking collectives  25.1 us (2%)
    all_gather x1, waiting for transfers between devices, per_device(): gathered = lax.all_gather(piece, ('chan', 'tm'), axis=0, tiled=False)  1440 us
  transfers between devices with their start and end apart: 2, of which 2 were waited for; matrix products, arithmetic and copies ran while one was open for 0% of the time, Pallas kernels for 0%

profile of v1, /device:TPU:27, one launch (start us, length us, event | category | flops | bytes accessed | tf_op | source)
XLA Modules:
  0.0 1541.3 jit_solution(14987250532775447190)
XLA Ops:
  6.5 0.0 all-gather.3.cloned.1.call-start
  6.5 0.8 slice.3
  7.4 4.0 collective-permute-start
  11.4 0.7 rev.3
  12.1 0.1 reshape.28
  12.2 0.4 convolution_bitcast_fusion
  12.6 6.6 collective-permute-done
  19.2 1.6 multiply_reduce_fusion
  20.8 25.1 %psum.7 = f32[64,1]{0,1:T(1,128)S(1)} all-reduce(f32[64,1]{0,1:T(1,128)S(1)} %bitcast.27), channel_id=1, replica_groups=mesh['chan'=32,'tm'=16] {'tm'}, use_global_device_ids=true, to_apply=%region_1.0 | all-reduce | flops 64 | bytes 512 | tf_op jit(solution)/shard_map/psum | solution.py:49
  45.9 0.7 divide_convert_fusion
  46.6 0.0 all-gather.3.cloned.1.call-update
  46.6 0.7 fusion.7
  47.3 0.1 broadcast_in_dim.8
  47.4 0.1 mul.40
  47.5 1440.8 %all-gather.3.cloned.1.call-done = bf16[32768,128]{1,0:T(8,128)(2,1)} async-done(((bf16[64,128]{1,0:T(8,128)(2,1)}), bf16[32768,128]{1,0:T(8,128)(2,1)}) %all-gather.3.cloned.1.call-update) | async-done | bytes 8388624 | tf_op jit(solution)/shard_map/all_gather | solution.py:53
  1488.3 23.0 %copy.6 = bf16[32,16,64,128]{3,1,2,0:T(8,128)(2,1)} copy(bf16[32,16,64,128]{3,2,1,0:T(8,128)(2,1)} %bitcast.26) | data formatting | bytes 16777216 | tf_op jit(solution)/shard_map/reshape | solution.py:54
  1511.3 10.9 copy.12
  1522.2 1.0 constant_dynamic-slice_fusion.1
  1523.1 0.2 dynamic-slice_dynamic-update-slice_fusion.7
  1523.3 0.2 dynamic-slice_dynamic-update-slice_fusion.6
  1523.5 0.2 dynamic-slice_dynamic-update-slice_fusion.5
  1523.6 0.2 dynamic-slice_dynamic-update-slice_fusion.4
  1523.8 0.2 dynamic-slice_dynamic-update-slice_fusion.3
  1524.0 0.2 dynamic-slice_dynamic-update-slice_fusion.2
  1524.1 0.2 dynamic-slice_dynamic-update-slice_fusion.1
  1524.3 0.2 dynamic-slice_dynamic-update-slice_fusion
  1524.4 10.0 convolution_multiply_fusion
  (1 shorter events, 0.0 us)
Async XLA Ops:
  6.5 1481.7 %all-gather.3.cloned.1.call-start = ((), (), s32[]{:S(2)}) async-start(), calls=%async_computation | async-start | bytes 8404992 | tf_op jit(solution)/shard_map/all_gather | solution.py:53
  7.4 11.8 collective-permute-start
Sparse Core Ops, SparseCore 0:
  46.7 1441.4 all-gather.2

commit v2 on v1

--- a/solution.py
+++ b/solution.py
@@ -43,21 +43,15 @@
     tm_parts = lax.axis_size("tm")
     decimated = decimate(raw_strain, fir_taps)
     rounded = decimated.astype(jnp.bfloat16)
-    local_span = rounded.shape[1]
-    samples = local_span * tm_parts
-    values = rounded.astype(jnp.float32)
-    square_sum = lax.psum(jnp.sum(values * values, axis=1, keepdims=True), "tm")
-    root = jnp.sqrt(square_sum / samples + 1e-06)
-    piece = (values / root).astype(jnp.bfloat16)
+    gathered = lax.all_gather(rounded, "tm", axis=1, tiled=True)
+    samples = gathered.shape[1]
+    full_values = gathered.astype(jnp.float32)
+    root_whole = jnp.sqrt(jnp.mean(full_values * full_values, axis=1, keepdims=True) + 1e-06)
+    own = (full_values / root_whole).astype(jnp.bfloat16)
+    whole = lax.all_gather(own, "chan", axis=0, tiled=True)
 
-    gathered = lax.all_gather(piece, ("chan", "tm"), axis=0, tiled=False)
-    gathered = gathered.reshape(chan_parts, tm_parts, channel_rows, local_span)
-    whole = gathered.transpose(0, 2, 1, 3).reshape(chan_parts * channel_rows, samples)
-
-    chan_index = lax.axis_index("chan")
     lag_count = LAGS // tm_parts
     lag_base = lax.axis_index("tm") * lag_count
-    own = lax.dynamic_slice_in_dim(whole, chan_index * channel_rows, channel_rows, 0)
     reach = LAGS + lag_count
     padded = jnp.pad(own, ((0, 0), (reach, 0)))
     shifted = [
@@ -68,7 +62,7 @@
     product = lax.dot_general(
         stacked, whole, (((1,), (1,)), ((), ())), preferred_element_type=jnp.float32
     )
-    mask_row = lax.dynamic_index_in_dim(block_mask, chan_index, 0, keepdims=False)
+    mask_row = lax.dynamic_index_in_dim(block_mask, lax.axis_index("chan"), 0, keepdims=False)
     weights = jnp.repeat(mask_row, channel_rows).astype(jnp.float32) * (1.0 / math.sqrt(samples))
     return (product * weights[None, :]).reshape(lag_count, channel_rows, chan_parts * channel_rows)
 

time: 1540 us -> 152 us (0.10)
  the two profiles are of different devices: /device:TPU:27 before, /device:TPU:17 now
where the time goes in v2:
time: 152 us
  waiting for transfers between devices  82.2 us (54%)
  blocking collectives  33.4 us (22%)
  between operations  13.5 us (9%)
  matrix products  11.3 us (7%)
  local copies, waits for them, and re-layouts  5.87 us (4%)
  starting transfers between devices  3.99 us (3%)
  other arithmetic  1.73 us (1%)
    all_gather x1, waiting for transfers between devices, per_device(): whole = lax.all_gather(own, 'chan', axis=0, tiled=True)  82.2 us
    all_gather x1, blocking collectives, per_device(): gathered = lax.all_gather(rounded, 'tm', axis=1, tiled=True)  33.4 us
    dot_general x1, matrix products, per_device(): lax.dot_general(stacked, whole, (((1,), (1,)), ((), ())), preferred_eleme...  9.44 us
    ppermute x1, starting transfers between devices, from_behind(): lax.ppermute(value, axis, [(source, source + steps) for source in range(f...  3.99 us
    unnamed x9, local copies, waits for them, and re-layouts  3.91 us
  transfers between devices with their start and end apart: 2, of which 1 were waited for; matrix products, arithmetic and copies ran while one was open for 4% of the time, Pallas kernels for 0%

profile of v2, /device:TPU:17, one launch (start us, length us, event | category | flops | bytes accessed | tf_op | source)
XLA Modules:
  0.0 152.1 jit_solution(13342266144570115283)
XLA Ops:
  6.5 0.0 all-gather.2.cloned.1.call-start
  6.5 0.8 slice.3
  7.4 4.0 %collective-permute-start = (f32[64,56]{1,0:T(8,128)S(1)}, f32[64,56]{1,0:T(8,128)S(1)}, u32[]{:S(2)}, u32[]{:S(2)}) collective-permute-start(f32[64,56]{1,0:T(8,128)S(1)} %slice.3), channel_id=1, source_target_pairs={{0,1},{1,2},{2,3},{3,4},{4,5},{5,6},{6,7},{7,8},{8,9},{9,10},{10,1... | collective-permute-start | bytes 43016 | tf_op jit(solution)/shard_map/ppermute | solution.py:16
  11.4 0.7 rev.3
  12.1 0.1 reshape.30
  12.2 0.4 convolution_bitcast_fusion
  12.6 0.0 collective-permute-done
  12.7 1.5 convolution_convert_fusion
  14.1 33.4 %all_gather.6 = bf16[64,2048]{1,0:T(8,128)(2,1)S(1)} all-gather(bf16[64,128]{1,0:T(8,128)(2,1)S(1)} %convolution_convert_fusion), channel_id=1, replica_groups=mesh['chan'=32,'tm'=16] {'tm'}, dimensions={1}, use_global_device_ids=true | all-gather | bytes 278528 | tf_op jit(solution)/shard_map/all_gather | solution.py:46
  47.5 0.2 fusion
  47.7 0.8 fusion.1
  48.5 0.0 copy-start
  48.5 0.0 all-gather.2.cloned.1.call-update
  48.6 0.7 fusion.8
  49.3 0.1 broadcast_in_dim.2
  49.4 0.1 mul.36
  49.5 1.1 dynamic-slice_dynamic-update-slice_fusion.7
  50.5 1.1 dynamic-slice_dynamic-update-slice_fusion.6
  51.7 1.1 dynamic-slice_dynamic-update-slice_fusion.5
  52.8 0.0 copy-done
  52.8 0.2 dynamic-slice_dynamic-update-slice_fusion.4
  52.9 0.2 dynamic-slice_dynamic-update-slice_fusion.3
  53.1 0.2 dynamic-slice_dynamic-update-slice_fusion.2
  53.3 0.2 dynamic-slice_dynamic-update-slice_fusion.1
  53.4 0.2 dynamic-slice_dynamic-update-slice_fusion
  53.6 82.2 %all-gather.2.cloned.1.call-done = bf16[2048,2048]{1,0:T(8,128)(2,1)} async-done(((bf16[64,2048]{1,0:T(8,128)(2,1)}), bf16[2048,2048]{1,0:T(8,128)(2,1)}) %all-gather.2.cloned.1.call-update) | async-done | bytes 8388624 | tf_op jit(solution)/shard_map/all_gather | solution.py:51
  135.8 9.4 %convolution_multiply_fusion = f32[512,2048]{1,0:T(8,128)} fusion(bf16[512,2048]{1,0:T(8,128)(2,1)S(1)} %dynamic-slice_dynamic-update-slice_fusion, bf16[2048,2048]{1,0:T(8,128)(2,1)} %all-gather.2.cloned.1.call-done, f32[2048]{0:T(1024)S(1)} %mul.36), kind=kOutput, calls=%fused_computation | convolution fusion | flops 4296015872 | bytes 14688256 | tf_op jit(solution)/shard_map/dot_general | solution.py:62
  (1 shorter events, 0.0 us)
Async XLA Ops:
  6.5 129.2 %all-gather.2.cloned.1.call-start = ((), (), s32[]{:S(2)}) async-start(), calls=%async_computation | async-start | bytes 8650752 | tf_op jit(solution)/shard_map/all_gather | solution.py:51
  7.4 5.3 %collective-permute-start = (f32[64,56]{1,0:T(8,128)S(1)}, f32[64,56]{1,0:T(8,128)S(1)}, u32[]{:S(2)}, u32[]{:S(2)}) collective-permute-start(f32[64,56]{1,0:T(8,128)S(1)} %slice.3), channel_id=1, source_target_pairs={{0,1},{1,2},{2,3},{3,4},{4,5},{5,6},{6,7},{7,8},{8,9},{9,10},{10,1... | collective-permute-start | bytes 43016 | tf_op jit(solution)/shard_map/ppermute | solution.py:16
  48.5 4.2 %copy-start = (bf16[64,2048]{1,0:T(8,128)(2,1)S(1)}, bf16[64,2048]{1,0:T(8,128)(2,1)}, u32[]{:S(2)}) copy-start(bf16[64,2048]{1,0:T(8,128)(2,1)} %fusion.1) | copy-start | bytes 786436
Sparse Core Ops, SparseCore 0:
  48.7 87.0 all-gather.1

commit v3 on v2

--- a/solution.py
+++ b/solution.py
@@ -37,13 +37,19 @@
     )
 
 
+def gather_time(piece, parts):
+    repeated = jnp.broadcast_to(piece[None], (parts,) + piece.shape)
+    in_order = lax.all_to_all(repeated, "tm", 0, 0, tiled=False)
+    return in_order.transpose(1, 0, 2).reshape(piece.shape[0], parts * piece.shape[1])
+
+
 def per_device(raw_strain, fir_taps, block_mask):
     channel_rows = raw_strain.shape[0]
     chan_parts = lax.axis_size("chan")
     tm_parts = lax.axis_size("tm")
     decimated = decimate(raw_strain, fir_taps)
     rounded = decimated.astype(jnp.bfloat16)
-    gathered = lax.all_gather(rounded, "tm", axis=1, tiled=True)
+    gathered = gather_time(rounded, tm_parts)
     samples = gathered.shape[1]
     full_values = gathered.astype(jnp.float32)
     root_whole = jnp.sqrt(jnp.mean(full_values * full_values, axis=1, keepdims=True) + 1e-06)

time: 152 us -> 134 us (0.88)
  blocking collectives: 33.4 us -> 19.2 us
  waiting for transfers between devices: 82.2 us -> 78.5 us
    all_gather x1 -> x0, blocking collectives: 33.4 us -> none  [per_device(): gathered = lax.all_gather(rounded, 'tm', axis=1, tiled=True)]
    all_to_all x0 -> x1, blocking collectives: none -> 19.2 us  [gather_time(): in_order = lax.all_to_all(repeated, 'tm', 0, 0, tiled=False)]
    all_gather x1, waiting for transfers between devices: 82.2 us -> 78.4 us  [per_device(): whole = lax.all_gather(own, 'chan', axis=0, tiled=True)]
  transfers between devices with their start and end apart: 2 -> 2, of which waited for: 1 -> 1; matrix products, arithmetic and copies ran while one was open for 4% -> 5% of each run, Pallas kernels for 0% -> 0%
where the time goes in v3:
time: 134 us
  waiting for transfers between devices  78.5 us (59%)
  blocking collectives  19.2 us (14%)
  between operations  13.5 us (10%)
  matrix products  11.3 us (8%)
  local copies, waits for them, and re-layouts  5.91 us (4%)
  starting transfers between devices  3.99 us (3%)
  other arithmetic  1.73 us (1%)
    all_gather x1, waiting for transfers between devices, per_device(): whole = lax.all_gather(own, 'chan', axis=0, tiled=True)  78.4 us
    all_to_all x1, blocking collectives, gather_time(): in_order = lax.all_to_all(repeated, 'tm', 0, 0, tiled=False)  19.2 us
    dot_general x1, matrix products, per_device(): lax.dot_general(stacked, whole, (((1,), (1,)), ((), ())), preferred_eleme...  9.44 us
    ppermute x1, starting transfers between devices, from_behind(): lax.ppermute(value, axis, [(source, source + steps) for source in range(f...  3.99 us
    unnamed x9, local copies, waits for them, and re-layouts  3.91 us
  transfers between devices with their start and end apart: 2, of which 1 were waited for; matrix products, arithmetic and copies ran while one was open for 5% of the time, Pallas kernels for 0%

profile of v3, /device:TPU:17, one launch (start us, length us, event | category | flops | bytes accessed | tf_op | source)
XLA Modules:
  0.0 134.1 jit_solution(18037135932674082787)
XLA Ops:
  6.5 0.0 all-gather.2.cloned.1.call-start
  6.5 0.8 slice.3
  7.4 4.0 %collective-permute-start = (f32[64,56]{1,0:T(8,128)S(1)}, f32[64,56]{1,0:T(8,128)S(1)}, u32[]{:S(2)}, u32[]{:S(2)}) collective-permute-start(f32[64,56]{1,0:T(8,128)S(1)} %slice.3), channel_id=1, source_target_pairs={{0,1},{1,2},{2,3},{3,4},{4,5},{5,6},{6,7},{7,8},{8,9},{9,10},{10,1... | collective-permute-start | bytes 43016 | tf_op jit(solution)/shard_map/ppermute | solution.py:16
  11.4 0.7 rev.3
  12.1 0.1 reshape.34
  12.2 0.4 convolution_bitcast_fusion
  12.6 0.0 collective-permute-done
  12.7 1.5 %convolution_convert_fusion = bf16[64,128]{1,0:T(8,128)(2,1)S(1)} fusion(f32[1080,128]{1,0:T(8,128)S(1)} %convolution_bitcast_fusion, f32[64,1024]{1,0:T(8,128)} %param.3, f32[64,56]{1,0:T(8,128)S(1)} %collective-permute-done), kind=kOutput, calls=%fused_computation.2 | convolution fusion | flops 106245632 | bytes 845824 | tf_op jit(solution)/shard_map/dot_general | solution.py:35
  14.2 19.2 %all_to_all.5 = bf16[16,64,128]{2,1,0:T(8,128)(2,1)S(1)} all-to-all(bf16[16,64,128]{2,1,0:T(8,128)(2,1)S(1)} %broadcast_in_dim.4), channel_id=1, replica_groups=mesh['chan'=32,'tm'=16] {'tm'}, dimensions={0} | all-to-all | bytes 524288 | tf_op jit(solution)/shard_map/all_to_all | solution.py:42
  33.3 0.2 fusion
  33.5 0.8 fusion.1
  34.3 0.0 copy-start
  34.3 0.0 all-gather.2.cloned.1.call-update
  34.4 0.7 fusion.8
  35.1 0.1 broadcast_in_dim.5
  35.2 0.1 mul.38
  35.2 1.1 dynamic-slice_dynamic-update-slice_fusion.7
  36.3 1.1 dynamic-slice_dynamic-update-slice_fusion.6
  37.4 1.1 dynamic-slice_dynamic-update-slice_fusion.5
  38.6 0.0 copy-done
  38.6 0.2 dynamic-slice_dynamic-update-slice_fusion.4
  38.7 0.2 dynamic-slice_dynamic-update-slice_fusion.3
  38.9 0.2 dynamic-slice_dynamic-update-slice_fusion.2
  39.0 0.2 dynamic-slice_dynamic-update-slice_fusion.1
  39.2 0.2 dynamic-slice_dynamic-update-slice_fusion
  39.4 78.4 %all-gather.2.cloned.1.call-done = bf16[2048,2048]{1,0:T(8,128)(2,1)} async-done(((bf16[64,2048]{1,0:T(8,128)(2,1)}), bf16[2048,2048]{1,0:T(8,128)(2,1)}) %all-gather.2.cloned.1.call-update) | async-done | bytes 8388624 | tf_op jit(solution)/shard_map/all_gather | solution.py:57
  117.8 9.4 %convolution_multiply_fusion = f32[512,2048]{1,0:T(8,128)} fusion(bf16[512,2048]{1,0:T(8,128)(2,1)S(1)} %dynamic-slice_dynamic-update-slice_fusion, bf16[2048,2048]{1,0:T(8,128)(2,1)} %all-gather.2.cloned.1.call-done, f32[2048]{0:T(1024)S(1)} %mul.38), kind=kOutput, calls=%fused_computation | convolution fusion | flops 4296015872 | bytes 14688256 | tf_op jit(solution)/shard_map/dot_general | solution.py:68
  (2 shorter events, 0.1 us)
Async XLA Ops:
  6.5 111.3 %all-gather.2.cloned.1.call-start = ((), (), s32[]{:S(2)}) async-start(), calls=%async_computation.1 | async-start | bytes 8650752 | tf_op jit(solution)/shard_map/all_gather | solution.py:57
  7.4 5.3 %collective-permute-start = (f32[64,56]{1,0:T(8,128)S(1)}, f32[64,56]{1,0:T(8,128)S(1)}, u32[]{:S(2)}, u32[]{:S(2)}) collective-permute-start(f32[64,56]{1,0:T(8,128)S(1)} %slice.3), channel_id=1, source_target_pairs={{0,1},{1,2},{2,3},{3,4},{4,5},{5,6},{6,7},{7,8},{8,9},{9,10},{10,1... | collective-permute-start | bytes 43016 | tf_op jit(solution)/shard_map/ppermute | solution.py:16
  34.3 4.2 %copy-start = (bf16[64,2048]{1,0:T(8,128)(2,1)S(1)}, bf16[64,2048]{1,0:T(8,128)(2,1)}, u32[]{:S(2)}) copy-start(bf16[64,2048]{1,0:T(8,128)(2,1)} %fusion.1) | copy-start | bytes 786436
Sparse Core Ops, SparseCore 0:
  34.5 83.2 all-gather.1

commit v4 on v3

--- a/solution.py
+++ b/solution.py
@@ -1,8 +1,11 @@
+import functools
 import math
 
 import jax
 import jax.numpy as jnp
 from jax import lax
+from jax.experimental import pallas as pl
+from jax.experimental.pallas import tpu as pltpu
 from jax.sharding import PartitionSpec as P
 
 DECIM = 8
@@ -43,6 +46,58 @@
     return in_order.transpose(1, 0, 2).reshape(piece.shape[0], parts * piece.shape[1])
 
 
+def correlate_kernel(mask_ref, stacked_ref, whole_ref, out_ref, *, scale, block_cols, mask_cols):
+    col = pl.program_id(0)
+    groups = block_cols // mask_cols
+    flags = [mask_ref[col * groups + group] for group in range(groups)]
+    live = flags[0] != 0
+    for flag in flags[1:]:
+        live = jnp.logical_or(live, flag != 0)
+
+    @pl.when(live)
+    def _():
+        product = lax.dot_general(
+            stacked_ref[...], whole_ref[...], (((1,), (1,)), ((), ())),
+            preferred_element_type=jnp.float32,
+        )
+        which = lax.broadcasted_iota(jnp.int32, (1, block_cols), 1) // mask_cols
+        weight = jnp.zeros((1, block_cols), jnp.float32)
+        for group, flag in enumerate(flags):
+            weight = jnp.where(which == group, flag.astype(jnp.float32) * scale, weight)
+        out_ref[...] = product * weight
+
+    @pl.when(jnp.logical_not(live))
+    def _():
+        out_ref[...] = jnp.zeros_like(out_ref)
+
+
+def correlate(stacked, whole, mask_row, scale, mask_cols):
+    rows, depth = stacked.shape
+    cols = whole.shape[0]
+    block_cols = 256
+    kernel = functools.partial(
+        correlate_kernel, scale=scale, block_cols=block_cols, mask_cols=mask_cols
+    )
+    return pl.pallas_call(
+        kernel,
+        out_shape=jax.ShapeDtypeStruct((rows, cols), jnp.float32),
+        grid_spec=pltpu.PrefetchScalarGridSpec(
+            num_scalar_prefetch=1,
+            grid=(cols // block_cols,),
+            in_specs=[
+                pl.BlockSpec((rows, depth), lambda col, mask: (0, 0)),
+                pl.BlockSpec((block_cols, depth), lambda col, mask: (col, 0)),
+            ],
+            out_specs=pl.BlockSpec((rows, block_cols), lambda col, mask: (0, col)),
+        ),
+        cost_estimate=pl.CostEstimate(
+            flops=2 * rows * depth * cols,
+            bytes_accessed=2 * rows * depth + 2 * cols * depth + 4 * rows * cols,
+            transcendentals=0,
+        ),
+    )(mask_row, stacked, whole)
+
+
 def per_device(raw_strain, fir_taps, block_mask):
     channel_rows = raw_strain.shape[0]
     chan_parts = lax.axis_size("chan")
@@ -65,12 +120,9 @@
         for step in range(lag_count)
     ]
     stacked = jnp.concatenate(shifted, axis=0)
-    product = lax.dot_general(
-        stacked, whole, (((1,), (1,)), ((), ())), preferred_element_type=jnp.float32
-    )
     mask_row = lax.dynamic_index_in_dim(block_mask, lax.axis_index("chan"), 0, keepdims=False)
-    weights = jnp.repeat(mask_row, channel_rows).astype(jnp.float32) * (1.0 / math.sqrt(samples))
-    return (product * weights[None, :]).reshape(lag_count, channel_rows, chan_parts * channel_rows)
+    product = correlate(stacked, whole, mask_row, 1.0 / math.sqrt(samples), channel_rows)
+    return product.reshape(lag_count, channel_rows, chan_parts * channel_rows)
 
 
 def solution(mesh):

time: 134 us -> 137 us (1.022)
  the two profiles are of different devices: /device:TPU:17 before, /device:TPU:11 now
where the time goes in v4:
time: 137 us; the launch traced here: 136 us
  waiting for transfers between devices  85.6 us (62%)
  between operations  13.5 us (10%)
  blocking collectives  12.4 us (9%)
  Pallas kernels  11.7 us (9%)
  local copies, waits for them, and re-layouts  6.3 us (5%)
  starting transfers between devices  4 us (3%)
  matrix products  1.89 us (1%)
    all_gather x1, waiting for transfers between devices, per_device(): whole = lax.all_gather(own, 'chan', axis=0, tiled=True)  79 us
    all_to_all x1, blocking collectives, gather_time(): in_order = lax.all_to_all(repeated, 'tm', 0, 0, tiled=False)  12.4 us
    pallas_call x1, Pallas kernels, correlate(): pl.pallas_call(kernel, out_shape=jax.ShapeDtypeStruct((rows, cols), jnp.f...  11.7 us
    ppermute x1, waiting for transfers between devices, from_behind(): lax.ppermute(value, axis, [(source, source + steps) for source in range(f...  6.57 us
    ppermute x1, starting transfers between devices, from_behind(): lax.ppermute(value, axis, [(source, source + steps) for source in range(f...  3.99 us
    unnamed x13, local copies, waits for them, and re-layouts  3.92 us
  transfers between devices with their start and end apart: 2, of which 2 were waited for; matrix products, arithmetic and copies ran while one was open for 4% of the time, Pallas kernels for 0%

profile of v4, /device:TPU:11, one launch (start us, length us, event | category | flops | bytes accessed | tf_op | source)
XLA Modules:
  0.0 136.3 jit_solution(2110144172373687871)
XLA Ops:
  6.5 0.0 copy-start
  6.5 0.0 all-gather.2.cloned.1.call-start
  6.5 0.8 slice.3
  7.4 4.0 %collective-permute-start = (f32[64,56]{1,0:T(8,128)S(1)}, f32[64,56]{1,0:T(8,128)S(1)}, u32[]{:S(2)}, u32[]{:S(2)}) collective-permute-start(f32[64,56]{1,0:T(8,128)S(1)} %slice.3), channel_id=1, source_target_pairs={{0,1},{1,2},{2,3},{3,4},{4,5},{5,6},{6,7},{7,8},{8,9},{9,10},{10,1... | collective-permute-start | bytes 43016 | tf_op jit(solution)/shard_map/ppermute | solution.py:19
  11.4 0.7 rev.3
  12.1 0.1 reshape.21
  12.2 0.4 convolution_bitcast_fusion
  12.7 6.6 %collective-permute-done = f32[64,56]{1,0:T(8,128)S(1)} collective-permute-done((f32[64,56]{1,0:T(8,128)S(1)}, f32[64,56]{1,0:T(8,128)S(1)}, u32[]{:S(2)}, u32[]{:S(2)}) %collective-permute-start) | collective-permute-done | bytes 14368 | tf_op jit(solution)/shard_map/ppermute | solution.py:19
  19.2 1.5 %convolution_convert_fusion = bf16[64,128]{1,0:T(8,128)(2,1)S(1)} fusion(f32[1080,128]{1,0:T(8,128)S(1)} %convolution_bitcast_fusion, f32[64,1024]{1,0:T(8,128)} %param.3, f32[64,56]{1,0:T(8,128)S(1)} %collective-permute-done), kind=kOutput, calls=%fused_computation.1 | convolution fusion | flops 106245632 | bytes 845824 | tf_op jit(solution)/shard_map/dot_general | solution.py:38
  20.7 12.4 %all_to_all.5 = bf16[16,64,128]{2,1,0:T(8,128)(2,1)S(1)} all-to-all(bf16[16,64,128]{2,1,0:T(8,128)(2,1)S(1)} %broadcast_in_dim.2), channel_id=1, replica_groups=mesh['chan'=32,'tm'=16] {'tm'}, dimensions={0} | all-to-all | bytes 524288 | tf_op jit(solution)/shard_map/all_to_all | solution.py:45
  33.1 0.2 fusion
  33.3 0.8 fusion.1
  34.1 0.0 copy-start.1
  34.1 0.0 all-gather.2.cloned.1.call-update
  34.1 0.0 copy-done
  34.2 0.5 fusion.6.mask_ref
  34.7 1.1 dynamic-slice_dynamic-update-slice_fusion.7
  35.8 1.1 dynamic-slice_dynamic-update-slice_fusion.6
  36.9 1.1 dynamic-slice_dynamic-update-slice_fusion.5
  38.0 0.0 copy-done.1
  38.0 0.2 dynamic-slice_dynamic-update-slice_fusion.4
  38.1 0.2 dynamic-slice_dynamic-update-slice_fusion.3
  38.3 0.2 dynamic-slice_dynamic-update-slice_fusion.2
  38.5 0.2 dynamic-slice_dynamic-update-slice_fusion.1
  38.6 0.2 dynamic-slice_dynamic-update-slice_fusion.stacked_ref
  38.8 0.0 copy-start.2
  38.8 79.0 %all-gather.2.cloned.1.call-done.whole_ref = bf16[2048,2048]{1,0:T(8,128)(2,1)} async-done(((bf16[64,2048]{1,0:T(8,128)(2,1)}), bf16[2048,2048]{1,0:T(8,128)(2,1)}) %all-gather.2.cloned.1.call-update) | async-done | bytes 8388624 | tf_op jit(solution)/shard_map/all_gather | solution.py:112
  117.8 0.0 copy-done.2
  117.8 11.7 %shard_map.37 = f32[512,2048]{1,0:T(8,128)} custom-call(s32[32]{0:T(128)} %fusion.6.mask_ref, bf16[512,2048]{1,0:T(8,128)(2,1)} %copy-done.2, bf16[2048,2048]{1,0:T(8,128)(2,1)} %all-gather.2.cloned.1.call-done.whole_ref), custom_call_target="tpu_custom_call" | custom-call | flops 4294967296 | bytes 14680064 | tf_op jit(solution)/shard_map/pallas_call | solution.py:81
  (2 shorter events, 0.1 us)
Async XLA Ops:
  6.5 27.6 %copy-start = (s32[32,32]{1,0:T(8,128)S(1)}, s32[32,32]{1,0:T(8,128)}, u32[]{:S(2)}) copy-start(s32[32,32]{1,0:T(8,128)} %param.5) | copy-start | bytes 12292
  6.5 111.3 %all-gather.2.cloned.1.call-start = ((), (), s32[]{:S(2)}) async-start(), calls=%async_computation.1 | async-start | bytes 8650752 | tf_op jit(solution)/shard_map/all_gather | solution.py:112
  7.4 11.8 %collective-permute-start = (f32[64,56]{1,0:T(8,128)S(1)}, f32[64,56]{1,0:T(8,128)S(1)}, u32[]{:S(2)}, u32[]{:S(2)}) collective-permute-start(f32[64,56]{1,0:T(8,128)S(1)} %slice.3), channel_id=1, source_target_pairs={{0,1},{1,2},{2,3},{3,4},{4,5},{5,6},{6,7},{7,8},{8,9},{9,10},{10,1... | collective-permute-start | bytes 43016 | tf_op jit(solution)/shard_map/ppermute | solution.py:19
  34.1 3.9 %copy-start.1 = (bf16[64,2048]{1,0:T(8,128)(2,1)S(1)}, bf16[64,2048]{1,0:T(8,128)(2,1)}, u32[]{:S(2)}) copy-start(bf16[64,2048]{1,0:T(8,128)(2,1)} %fusion.1) | copy-start | bytes 786436
  38.8 79.0 %copy-start.2 = (bf16[512,2048]{1,0:T(8,128)(2,1)}, bf16[512,2048]{1,0:T(8,128)(2,1)S(1)}, u32[]{:S(2)}) copy-start(bf16[512,2048]{1,0:T(8,128)(2,1)S(1)} %dynamic-slice_dynamic-update-slice_fusion.stacked_ref) | copy-start | bytes 6291460
Sparse Core Ops, SparseCore 0:
  34.3 83.5 all-gather.1

commit v5 on v2

--- a/solution.py
+++ b/solution.py
@@ -10,18 +10,7 @@
 LAGS = 128
 
 
-def from_behind(value, axis, steps):
-    count = lax.axis_size(axis)
-    first, last = (max(0, -steps), min(count, count - steps))
-    return lax.ppermute(value, axis, [(source, source + steps) for source in range(first, last)])
-
-
-def decimate(raw_strain, fir_taps):
-    time_span = raw_strain.shape[1]
-    margin = TAPS - DECIM
-    earlier = from_behind(raw_strain[:, time_span - margin :], "tm", 1)
-    extended = jnp.concatenate([earlier, raw_strain], axis=1)
-    outputs = time_span // DECIM
+def filter_matrix_of(fir_taps, outputs):
     tap_blocks = TAPS // DECIM
     frames = outputs + tap_blocks - 1
     tap_table = fir_taps[::-1].reshape(tap_blocks, DECIM)
@@ -31,21 +20,46 @@
     ) == lax.broadcasted_iota(jnp.int32, shape_three, 2)
     one_hot = matches.astype(jnp.float32)
     filter_matrix = jnp.einsum("mtj,jr->mrt", one_hot, tap_table, precision=lax.Precision.HIGHEST)
-    filter_matrix = filter_matrix.reshape(frames * DECIM, outputs)
-    return jnp.dot(
-        extended, filter_matrix, precision=lax.Precision.HIGHEST, preferred_element_type=jnp.float32
+    return filter_matrix.reshape(frames * DECIM, outputs)
+
+
+def decimate_parts(raw_strain, fir_taps):
+    time_span = raw_strain.shape[1]
+    margin = TAPS - DECIM
+    outputs = time_span // DECIM
+    filter_matrix = filter_matrix_of(fir_taps, outputs)
+    main = jnp.dot(
+        raw_strain, filter_matrix[margin:], precision=lax.Precision.HIGHEST,
+        preferred_element_type=jnp.float32,
     )
+    carry = jnp.dot(
+        raw_strain[:, time_span - margin :], filter_matrix[:margin, :DECIM],
+        precision=lax.Precision.HIGHEST, preferred_element_type=jnp.float32,
+    )
+    return main, carry
+
+
+def gather_time(main, carry, parts):
+    piece = jnp.concatenate([main, carry], axis=1)
+    repeated = jnp.broadcast_to(piece[None], (parts,) + piece.shape)
+    arrived = lax.all_to_all(repeated, "tm", 0, 0, tiled=False)
+    span = main.shape[1]
+    mains = arrived[:, :, :span]
+    carries = arrived[:, :, span:]
+    before = jnp.concatenate([jnp.zeros_like(carries[:1]), carries[:-1]], axis=0)
+    before = jnp.pad(before, ((0, 0), (0, 0), (0, span - carries.shape[2])))
+    decimated = mains + before
+    return decimated.transpose(1, 0, 2).reshape(main.shape[0], parts * span)
 
 
 def per_device(raw_strain, fir_taps, block_mask):
     channel_rows = raw_strain.shape[0]
     chan_parts = lax.axis_size("chan")
     tm_parts = lax.axis_size("tm")
-    decimated = decimate(raw_strain, fir_taps)
-    rounded = decimated.astype(jnp.bfloat16)
-    gathered = lax.all_gather(rounded, "tm", axis=1, tiled=True)
-    samples = gathered.shape[1]
-    full_values = gathered.astype(jnp.float32)
+    main, carry = decimate_parts(raw_strain, fir_taps)
+    decimated = gather_time(main, carry, tm_parts)
+    full_values = lax.reduce_precision(decimated, exponent_bits=8, mantissa_bits=7)
+    samples = full_values.shape[1]
     root_whole = jnp.sqrt(jnp.mean(full_values * full_values, axis=1, keepdims=True) + 1e-06)
     own = (full_values / root_whole).astype(jnp.bfloat16)
     whole = lax.all_gather(own, "chan", axis=0, tiled=True)

time: 152 us -> 147 us (0.967)
  starting transfers between devices: 3.99 us -> 0.01 us
  waiting for transfers between devices: 82.2 us -> 78.9 us
  blocking collectives: 33.4 us -> 35.5 us
    all_to_all x0 -> x1, blocking collectives: none -> 35.5 us  [gather_time(): arrived = lax.all_to_all(repeated, 'tm', 0, 0, tiled=False)]
    all_gather x1 -> x0, blocking collectives: 33.4 us -> none  [per_device(): gathered = lax.all_gather(rounded, 'tm', axis=1, tiled=True)]
    ppermute x1 -> x0, starting transfers between devices: 3.99 us -> none  [from_behind(): lax.ppermute(value, axis, [(source, source + steps) for source in range(f...]
    all_gather x1, waiting for transfers between devices: 82.2 us -> 78.9 us  [per_device(): whole = lax.all_gather(own, 'chan', axis=0, tiled=True)]
  transfers between devices with their start and end apart: 2 -> 1, of which waited for: 1 -> 1; matrix products, arithmetic and copies ran while one was open for 4% -> 3% of each run, Pallas kernels for 0% -> 0%
where the time goes in v5:
time: 147 us
  waiting for transfers between devices  78.9 us (54%)
  blocking collectives  35.5 us (24%)
  between operations  13.5 us (9%)
  matrix products  12.3 us (8%)
  local copies, waits for them, and re-layouts  5.17 us (4%)
  other arithmetic  1.77 us (1%)
    all_gather x1, waiting for transfers between devices, per_device(): whole = lax.all_gather(own, 'chan', axis=0, tiled=True)  78.9 us
    all_to_all x1, blocking collectives, gather_time(): arrived = lax.all_to_all(repeated, 'tm', 0, 0, tiled=False)  35.5 us
    dot_general x1, matrix products, per_device(): lax.dot_general(stacked, whole, (((1,), (1,)), ((), ())), preferred_eleme...  9.44 us
    unnamed x9, local copies, waits for them, and re-layouts  3.91 us
  transfers between devices with their start and end apart: 1, of which 1 were waited for; matrix products, arithmetic and copies ran while one was open for 3% of the time, Pallas kernels for 0%

profile of v5, /device:TPU:17, one launch (start us, length us, event | category | flops | bytes accessed | tf_op | source)
XLA Modules:
  0.0 147.1 jit_solution(445718380649823180)
XLA Ops:
  6.5 0.0 all-gather.2.cloned.1.call-start
  6.5 0.7 rev.3
  7.3 0.1 reshape.34
  7.4 0.4 fusion
  7.8 1.4 convolution_bitcast_fusion.1
  9.2 1.0 convolution_bitcast_fusion
  10.2 0.1 broadcast_in_dim.4
  10.3 35.5 %all_to_all.5 = f32[16,64,136]{2,1,0:T(8,128)S(1)} all-to-all(f32[16,64,136]{2,1,0:T(8,128)S(1)} %broadcast_in_dim.4), channel_id=1, replica_groups=mesh['chan'=32,'tm'=16] {'tm'}, dimensions={0} | all-to-all | bytes 1114112 | tf_op jit(solution)/shard_map/all_to_all | solution.py:45
  45.8 0.2 multiply_reduce_fusion
  46.0 0.8 fusion.1
  46.9 0.0 copy-start
  46.9 0.0 all-gather.2.cloned.1.call-update
  46.9 0.7 fusion.9
  47.6 0.1 broadcast_in_dim.5
  47.7 0.1 mul.38
  47.8 1.1 dynamic-slice_dynamic-update-slice_fusion.7
  48.9 1.1 dynamic-slice_dynamic-update-slice_fusion.6
  50.0 1.1 dynamic-slice_dynamic-update-slice_fusion.5
  51.1 0.0 copy-done
  51.1 0.2 dynamic-slice_dynamic-update-slice_fusion.4
  51.3 0.2 dynamic-slice_dynamic-update-slice_fusion.3
  51.4 0.2 dynamic-slice_dynamic-update-slice_fusion.2
  51.6 0.2 dynamic-slice_dynamic-update-slice_fusion.1
  51.7 0.2 dynamic-slice_dynamic-update-slice_fusion
  51.9 78.9 %all-gather.2.cloned.1.call-done = bf16[2048,2048]{1,0:T(8,128)(2,1)} async-done(((bf16[64,2048]{1,0:T(8,128)(2,1)}), bf16[2048,2048]{1,0:T(8,128)(2,1)}) %all-gather.2.cloned.1.call-update) | async-done | bytes 8388624 | tf_op jit(solution)/shard_map/all_gather | solution.py:65
  130.8 9.4 %convolution_multiply_fusion = f32[512,2048]{1,0:T(8,128)} fusion(bf16[512,2048]{1,0:T(8,128)(2,1)S(1)} %dynamic-slice_dynamic-update-slice_fusion, bf16[2048,2048]{1,0:T(8,128)(2,1)} %all-gather.2.cloned.1.call-done, f32[2048]{0:T(1024)S(1)} %mul.38), kind=kOutput, calls=%fused_computation | convolution fusion | flops 4296015872 | bytes 14688256 | tf_op jit(solution)/shard_map/dot_general | solution.py:76
  (3 shorter events, 0.1 us)
Async XLA Ops:
  6.5 124.3 %all-gather.2.cloned.1.call-start = ((), (), s32[]{:S(2)}) async-start(), calls=%async_computation.1 | async-start | bytes 8650752 | tf_op jit(solution)/shard_map/all_gather | solution.py:65
  46.9 4.2 %copy-start = (bf16[64,2048]{1,0:T(8,128)(2,1)S(1)}, bf16[64,2048]{1,0:T(8,128)(2,1)}, u32[]{:S(2)}) copy-start(bf16[64,2048]{1,0:T(8,128)(2,1)} %fusion.1) | copy-start | bytes 786436
Sparse Core Ops, SparseCore 0:
  47.0 83.7 all-gather.1

commit v6 on v3

--- a/solution.py
+++ b/solution.py
@@ -20,7 +20,6 @@
     time_span = raw_strain.shape[1]
     margin = TAPS - DECIM
     earlier = from_behind(raw_strain[:, time_span - margin :], "tm", 1)
-    extended = jnp.concatenate([earlier, raw_strain], axis=1)
     outputs = time_span // DECIM
     tap_blocks = TAPS // DECIM
     frames = outputs + tap_blocks - 1
@@ -32,9 +31,16 @@
     one_hot = matches.astype(jnp.float32)
     filter_matrix = jnp.einsum("mtj,jr->mrt", one_hot, tap_table, precision=lax.Precision.HIGHEST)
     filter_matrix = filter_matrix.reshape(frames * DECIM, outputs)
-    return jnp.dot(
-        extended, filter_matrix, precision=lax.Precision.HIGHEST, preferred_element_type=jnp.float32
+    main = jnp.dot(
+        raw_strain, filter_matrix[margin:], precision=lax.Precision.HIGHEST,
+        preferred_element_type=jnp.float32,
     )
+    head = jnp.dot(
+        earlier, filter_matrix[:margin, :DECIM], precision=lax.Precision.HIGHEST,
+        preferred_element_type=jnp.float32,
+    )
+    main = lax.optimization_barrier(main)
+    return main + jnp.pad(head, ((0, 0), (0, outputs - DECIM)))
 
 
 def gather_time(piece, parts):

time: 134 us -> 133 us (level)
  blocking collectives: 19.2 us -> 17.8 us
    all_to_all x1, blocking collectives: 19.2 us -> 17.8 us  [gather_time(): in_order = lax.all_to_all(repeated, 'tm', 0, 0, tiled=False)]
  transfers between devices with their start and end apart: 2 -> 2, of which waited for: 1 -> 1; matrix products, arithmetic and copies ran while one was open for 5% -> 6% of each run, Pallas kernels for 0% -> 0%
where the time goes in v6:
time: 133 us
  waiting for transfers between devices  78.5 us (59%)
  blocking collectives  17.8 us (13%)
  between operations  13.5 us (10%)
  matrix products  11.4 us (9%)
  local copies, waits for them, and re-layouts  5.91 us (4%)
  starting transfers between devices  3.99 us (3%)
  other arithmetic  1.74 us (1%)
    all_gather x1, waiting for transfers between devices, per_device(): whole = lax.all_gather(own, 'chan', axis=0, tiled=True)  78.4 us
    all_to_all x1, blocking collectives, gather_time(): in_order = lax.all_to_all(repeated, 'tm', 0, 0, tiled=False)  17.8 us
    dot_general x1, matrix products, per_device(): lax.dot_general(stacked, whole, (((1,), (1,)), ((), ())), preferred_eleme...  9.44 us
    ppermute x1, starting transfers between devices, from_behind(): lax.ppermute(value, axis, [(source, source + steps) for source in range(f...  3.99 us
    unnamed x9, local copies, waits for them, and re-layouts  3.91 us
  transfers between devices with their start and end apart: 2, of which 1 were waited for; matrix products, arithmetic and copies ran while one was open for 6% of the time, Pallas kernels for 0%

profile of v6, /device:TPU:17, one launch (start us, length us, event | category | flops | bytes accessed | tf_op | source)
XLA Modules:
  0.0 132.8 jit_solution(15168749672077511378)
XLA Ops:
  6.5 0.0 all-gather.2.cloned.1.call-start
  6.5 0.8 slice.15
  7.4 4.0 %collective-permute-start = (f32[64,56]{1,0:T(8,128)S(1)}, f32[64,56]{1,0:T(8,128)S(1)}, u32[]{:S(2)}, u32[]{:S(2)}) collective-permute-start(f32[64,56]{1,0:T(8,128)S(1)} %slice.15), channel_id=1, source_target_pairs={{0,1},{1,2},{2,3},{3,4},{4,5},{5,6},{6,7},{7,8},{8,9},{9,10},{10,1... | collective-permute-start | bytes 43016 | tf_op jit(solution)/shard_map/ppermute | solution.py:16
  11.4 0.7 rev.3
  12.1 0.1 reshape.35
  12.2 0.4 fusion
  12.6 1.4 %convolution_bitcast_fusion.1 = f32[64,128]{1,0:T(8,128)S(1)} fusion(f32[64,1024]{1,0:T(8,128)} %param.3, f32[135,8,128]{2,1,0:T(8,128)S(1)} %bitcast.28), kind=kOutput, calls=%fused_computation.2 | convolution fusion | flops 100663296 | bytes 819200 | tf_op jit(solution)/shard_map/dot_general | solution.py:34
  14.0 0.0 collective-permute-done
  14.0 0.2 convolution_bitcast_fusion
  14.3 17.8 %all_to_all.5 = bf16[16,64,128]{2,1,0:T(8,128)(2,1)S(1)} all-to-all(bf16[16,64,128]{2,1,0:T(8,128)(2,1)S(1)} %broadcast_in_dim.4), channel_id=1, replica_groups=mesh['chan'=32,'tm'=16] {'tm'}, dimensions={0} | all-to-all | bytes 524288 | tf_op jit(solution)/shard_map/all_to_all | solution.py:48
  32.1 0.2 fusion.1
  32.2 0.8 fusion.2
  33.1 0.0 copy-start
  33.1 0.0 all-gather.2.cloned.1.call-update
  33.1 0.7 fusion.7
  33.8 0.1 broadcast_in_dim.5
  33.9 0.1 mul.38
  34.0 1.1 dynamic-slice_dynamic-update-slice_fusion.7
  35.1 1.1 dynamic-slice_dynamic-update-slice_fusion.6
  36.2 1.1 dynamic-slice_dynamic-update-slice_fusion.5
  37.3 0.0 copy-done
  37.3 0.2 dynamic-slice_dynamic-update-slice_fusion.4
  37.5 0.2 dynamic-slice_dynamic-update-slice_fusion.3
  37.6 0.2 dynamic-slice_dynamic-update-slice_fusion.2
  37.8 0.2 dynamic-slice_dynamic-update-slice_fusion.1
  37.9 0.2 dynamic-slice_dynamic-update-slice_fusion
  38.1 78.4 %all-gather.2.cloned.1.call-done = bf16[2048,2048]{1,0:T(8,128)(2,1)} async-done(((bf16[64,2048]{1,0:T(8,128)(2,1)}), bf16[2048,2048]{1,0:T(8,128)(2,1)}) %all-gather.2.cloned.1.call-update) | async-done | bytes 8388624 | tf_op jit(solution)/shard_map/all_gather | solution.py:63
  116.5 9.4 %convolution_multiply_fusion = f32[512,2048]{1,0:T(8,128)} fusion(bf16[512,2048]{1,0:T(8,128)(2,1)S(1)} %dynamic-slice_dynamic-update-slice_fusion, bf16[2048,2048]{1,0:T(8,128)(2,1)} %all-gather.2.cloned.1.call-done, f32[2048]{0:T(1024)S(1)} %mul.38), kind=kOutput, calls=%fused_computation | convolution fusion | flops 4296015872 | bytes 14688256 | tf_op jit(solution)/shard_map/dot_general | solution.py:74
  (3 shorter events, 0.1 us)
Async XLA Ops:
  6.5 110.0 %all-gather.2.cloned.1.call-start = ((), (), s32[]{:S(2)}) async-start(), calls=%async_computation.1 | async-start | bytes 8650752 | tf_op jit(solution)/shard_map/all_gather | solution.py:63
  7.4 6.7 %collective-permute-start = (f32[64,56]{1,0:T(8,128)S(1)}, f32[64,56]{1,0:T(8,128)S(1)}, u32[]{:S(2)}, u32[]{:S(2)}) collective-permute-start(f32[64,56]{1,0:T(8,128)S(1)} %slice.15), channel_id=1, source_target_pairs={{0,1},{1,2},{2,3},{3,4},{4,5},{5,6},{6,7},{7,8},{8,9},{9,10},{10,1... | collective-permute-start | bytes 43016 | tf_op jit(solution)/shard_map/ppermute | solution.py:16
  33.1 4.2 %copy-start = (bf16[64,2048]{1,0:T(8,128)(2,1)S(1)}, bf16[64,2048]{1,0:T(8,128)(2,1)}, u32[]{:S(2)}) copy-start(bf16[64,2048]{1,0:T(8,128)(2,1)} %fusion.2) | copy-start | bytes 786436
Sparse Core Ops, SparseCore 0:
  33.2 83.2 all-gather.1

commit v7 on v6

--- a/solution.py
+++ b/solution.py
@@ -1,6 +1,7 @@
 import math
 
 import jax
+import numpy as np
 import jax.numpy as jnp
 from jax import lax
 from jax.sharding import PartitionSpec as P
@@ -23,13 +24,15 @@
     outputs = time_span // DECIM
     tap_blocks = TAPS // DECIM
     frames = outputs + tap_blocks - 1
-    tap_table = fir_taps[::-1].reshape(tap_blocks, DECIM)
+    tap_grid = fir_taps.reshape(tap_blocks, DECIM)
     shape_three = (frames, outputs, tap_blocks)
     matches = lax.broadcasted_iota(jnp.int32, shape_three, 0) - lax.broadcasted_iota(
         jnp.int32, shape_three, 1
-    ) == lax.broadcasted_iota(jnp.int32, shape_three, 2)
+    ) == tap_blocks - 1 - lax.broadcasted_iota(jnp.int32, shape_three, 2)
     one_hot = matches.astype(jnp.float32)
-    filter_matrix = jnp.einsum("mtj,jr->mrt", one_hot, tap_table, precision=lax.Precision.HIGHEST)
+    flip = jnp.asarray(np.eye(DECIM, dtype=np.float32)[::-1])
+    tap_table = jnp.dot(tap_grid, flip, precision=lax.Precision.HIGHEST)
+    filter_matrix = jnp.einsum("mta,ar->mrt", one_hot, tap_table, precision=lax.Precision.HIGHEST)
     filter_matrix = filter_matrix.reshape(frames * DECIM, outputs)
     main = jnp.dot(
         raw_strain, filter_matrix[margin:], precision=lax.Precision.HIGHEST,

time: 133 us -> 134 us (level)
  no operation moved by 1% of the time
where the time goes in v7:
time: 134 us
  waiting for transfers between devices  77.8 us (58%)
  blocking collectives  18.3 us (14%)
  between operations  13.5 us (10%)
  matrix products  12.3 us (9%)
  local copies, waits for them, and re-layouts  5.82 us (4%)
  starting transfers between devices  3.99 us (3%)
  other arithmetic  1.74 us (1%)
    all_gather x1, waiting for transfers between devices, per_device(): whole = lax.all_gather(own, 'chan', axis=0, tiled=True)  77.8 us
    all_to_all x1, blocking collectives, gather_time(): in_order = lax.all_to_all(repeated, 'tm', 0, 0, tiled=False)  18.3 us
    dot_general x1, matrix products, per_device(): lax.dot_general(stacked, whole, (((1,), (1,)), ((), ())), preferred_eleme...  9.44 us
    ppermute x1, starting transfers between devices, from_behind(): lax.ppermute(value, axis, [(source, source + steps) for source in range(f...  3.99 us
    unnamed x9, local copies, waits for them, and re-layouts  3.91 us
  transfers between devices with their start and end apart: 2, of which 1 were waited for; matrix products, arithmetic and copies ran while one was open for 6% of the time, Pallas kernels for 0%

profile of v7, /device:TPU:17, one launch (start us, length us, event | category | flops | bytes accessed | tf_op | source)
XLA Modules:
  0.0 133.6 jit_solution(5608337306212734672)
XLA Ops:
  6.5 0.0 all-gather.2.cloned.1.call-start
  6.5 0.8 slice.15
  7.4 4.0 %collective-permute-start = (f32[64,56]{1,0:T(8,128)S(1)}, f32[64,56]{1,0:T(8,128)S(1)}, u32[]{:S(2)}, u32[]{:S(2)}) collective-permute-start(f32[64,56]{1,0:T(8,128)S(1)} %slice.15), channel_id=1, source_target_pairs={{0,1},{1,2},{2,3},{3,4},{4,5},{5,6},{6,7},{7,8},{8,9},{9,10},{10,1... | collective-permute-start | bytes 43016 | tf_op jit(solution)/shard_map/ppermute | solution.py:17
  11.4 0.7 reshape.35
  12.1 0.9 convolution_bitcast_fusion.2
  13.0 0.4 fusion
  13.4 1.4 %convolution_bitcast_fusion.1 = f32[64,128]{1,0:T(8,128)S(1)} fusion(f32[64,1024]{1,0:T(8,128)} %param.4, f32[135,8,128]{2,1,0:T(8,128)S(1)} %bitcast.30), kind=kOutput, calls=%fused_computation.2 | convolution fusion | flops 100663296 | bytes 819200 | tf_op jit(solution)/shard_map/dot_general | solution.py:37
  14.8 0.0 collective-permute-done
  14.8 0.2 convolution_bitcast_fusion
  15.1 18.3 %all_to_all.5 = bf16[16,64,128]{2,1,0:T(8,128)(2,1)S(1)} all-to-all(bf16[16,64,128]{2,1,0:T(8,128)(2,1)S(1)} %broadcast_in_dim.4), channel_id=1, replica_groups=mesh['chan'=32,'tm'=16] {'tm'}, dimensions={0} | all-to-all | bytes 524288 | tf_op jit(solution)/shard_map/all_to_all | solution.py:51
  33.4 0.2 fusion.1
  33.6 0.8 fusion.2
  34.4 0.0 copy-start
  34.4 0.0 all-gather.2.cloned.1.call-update
  34.4 0.7 fusion.7
  35.2 0.1 broadcast_in_dim.5
  35.2 0.1 mul.38
  35.3 1.1 dynamic-slice_dynamic-update-slice_fusion.7
  36.4 1.1 dynamic-slice_dynamic-update-slice_fusion.6
  37.5 1.1 dynamic-slice_dynamic-update-slice_fusion.5
  38.6 0.0 copy-done
  38.6 0.2 dynamic-slice_dynamic-update-slice_fusion.4
  38.8 0.2 dynamic-slice_dynamic-update-slice_fusion.3
  39.0 0.2 dynamic-slice_dynamic-update-slice_fusion.2
  39.1 0.2 dynamic-slice_dynamic-update-slice_fusion.1
  39.3 0.2 dynamic-slice_dynamic-update-slice_fusion
  39.4 77.8 %all-gather.2.cloned.1.call-done = bf16[2048,2048]{1,0:T(8,128)(2,1)} async-done(((bf16[64,2048]{1,0:T(8,128)(2,1)}), bf16[2048,2048]{1,0:T(8,128)(2,1)}) %all-gather.2.cloned.1.call-update) | async-done | bytes 8388624 | tf_op jit(solution)/shard_map/all_gather | solution.py:66
  117.3 9.4 %convolution_multiply_fusion = f32[512,2048]{1,0:T(8,128)} fusion(bf16[512,2048]{1,0:T(8,128)(2,1)S(1)} %dynamic-slice_dynamic-update-slice_fusion, bf16[2048,2048]{1,0:T(8,128)(2,1)} %all-gather.2.cloned.1.call-done, f32[2048]{0:T(1024)S(1)} %mul.38), kind=kOutput, calls=%fused_computation | convolution fusion | flops 4296015872 | bytes 14688256 | tf_op jit(solution)/shard_map/dot_general | solution.py:77
  (4 shorter events, 0.1 us)
Async XLA Ops:
  6.5 110.7 %all-gather.2.cloned.1.call-start = ((), (), s32[]{:S(2)}) async-start(), calls=%async_computation.1 | async-start | bytes 8650752 | tf_op jit(solution)/shard_map/all_gather | solution.py:66
  7.4 7.5 %collective-permute-start = (f32[64,56]{1,0:T(8,128)S(1)}, f32[64,56]{1,0:T(8,128)S(1)}, u32[]{:S(2)}, u32[]{:S(2)}) collective-permute-start(f32[64,56]{1,0:T(8,128)S(1)} %slice.15), channel_id=1, source_target_pairs={{0,1},{1,2},{2,3},{3,4},{4,5},{5,6},{6,7},{7,8},{8,9},{9,10},{10,1... | collective-permute-start | bytes 43016 | tf_op jit(solution)/shard_map/ppermute | solution.py:17
  34.4 4.2 %copy-start = (bf16[64,2048]{1,0:T(8,128)(2,1)S(1)}, bf16[64,2048]{1,0:T(8,128)(2,1)}, u32[]{:S(2)}) copy-start(bf16[64,2048]{1,0:T(8,128)(2,1)} %fusion.2) | copy-start | bytes 786436
Sparse Core Ops, SparseCore 0:
  34.5 82.6 all-gather.1

commit v8 on v6

--- a/solution.py
+++ b/solution.py
@@ -19,7 +19,7 @@
 def decimate(raw_strain, fir_taps):
     time_span = raw_strain.shape[1]
     margin = TAPS - DECIM
-    earlier = from_behind(raw_strain[:, time_span - margin :], "tm", 1)
+    earlier = from_behind(raw_strain, "tm", 1)[:, time_span - margin :]
     outputs = time_span // DECIM
     tap_blocks = TAPS // DECIM
     frames = outputs + tap_blocks - 1

time: 133 us -> 137 us (1.030)
  blocking collectives: 17.8 us -> 20.1 us
  waiting for transfers between devices: 78.5 us -> 80.8 us
    ppermute x1, waiting for transfers between devices: 0.01 us -> 2.61 us  [from_behind(): lax.ppermute(value, axis, [(source, source + steps) for source in range(f...]
    all_to_all x1, blocking collectives: 17.8 us -> 20.1 us  [gather_time(): in_order = lax.all_to_all(repeated, 'tm', 0, 0, tiled=False)]
  transfers between devices with their start and end apart: 2 -> 2, of which waited for: 1 -> 2; matrix products, arithmetic and copies ran while one was open for 6% -> 6% of each run, Pallas kernels for 0% -> 0%
where the time goes in v8:
time: 137 us
  waiting for transfers between devices  80.8 us (59%)
  blocking collectives  20.1 us (15%)
  between operations  13.5 us (10%)
  matrix products  11.5 us (8%)
  local copies, waits for them, and re-layouts  5.08 us (4%)
  starting transfers between devices  4 us (3%)
  other arithmetic  1.74 us (1%)
    all_gather x1, waiting for transfers between devices, per_device(): whole = lax.all_gather(own, 'chan', axis=0, tiled=True)  78.2 us
    all_to_all x1, blocking collectives, gather_time(): in_order = lax.all_to_all(repeated, 'tm', 0, 0, tiled=False)  20.1 us
    dot_general x1, matrix products, per_device(): lax.dot_general(stacked, whole, (((1,), (1,)), ((), ())), preferred_eleme...  9.44 us
    ppermute x1, starting transfers between devices, from_behind(): lax.ppermute(value, axis, [(source, source + steps) for source in range(f...  4 us
    unnamed x9, local copies, waits for them, and re-layouts  3.91 us
  transfers between devices with their start and end apart: 2, of which 2 were waited for; matrix products, arithmetic and copies ran while one was open for 6% of the time, Pallas kernels for 0%

profile of v8, /device:TPU:17, one launch (start us, length us, event | category | flops | bytes accessed | tf_op | source)
XLA Modules:
  0.0 136.7 jit_solution(5792212175510648962)
XLA Ops:
  6.5 0.0 all-gather.2.cloned.1.call-start
  6.5 4.0 %collective-permute-start = (f32[64,1024]{1,0:T(8,128)}, f32[64,1024]{1,0:T(8,128)S(1)}, u32[]{:S(2)}, u32[]{:S(2)}) collective-permute-start(f32[64,1024]{1,0:T(8,128)} %param.3), channel_id=1, source_target_pairs={{0,1},{1,2},{2,3},{3,4},{4,5},{5,6},{6,7},{7,8},{8,9},{9,10},{10,1... | collective-permute-start | bytes 786440 | tf_op jit(solution)/shard_map/ppermute | solution.py:16
  10.5 0.7 rev.3
  11.3 0.1 reshape.35
  11.4 0.4 fusion
  11.8 1.4 %convolution_bitcast_fusion.1 = f32[64,128]{1,0:T(8,128)S(1)} fusion(f32[64,1024]{1,0:T(8,128)} %param.3, f32[135,8,128]{2,1,0:T(8,128)S(1)} %bitcast.27), kind=kOutput, calls=%fused_computation.2 | convolution fusion | flops 100663296 | bytes 819200 | tf_op jit(solution)/shard_map/dot_general | solution.py:34
  13.2 2.6 %collective-permute-done = f32[64,1024]{1,0:T(8,128)S(1)} collective-permute-done((f32[64,1024]{1,0:T(8,128)}, f32[64,1024]{1,0:T(8,128)S(1)}, u32[]{:S(2)}, u32[]{:S(2)}) %collective-permute-start) | collective-permute-done | bytes 262176 | tf_op jit(solution)/shard_map/ppermute | solution.py:16
  15.8 0.2 convolution_bitcast_fusion
  16.1 20.1 %all_to_all.5 = bf16[16,64,128]{2,1,0:T(8,128)(2,1)S(1)} all-to-all(bf16[16,64,128]{2,1,0:T(8,128)(2,1)S(1)} %broadcast_in_dim.4), channel_id=1, replica_groups=mesh['chan'=32,'tm'=16] {'tm'}, dimensions={0} | all-to-all | bytes 524288 | tf_op jit(solution)/shard_map/all_to_all | solution.py:48
  36.2 0.2 fusion.1
  36.4 0.8 fusion.2
  37.2 0.0 copy-start
  37.2 0.0 all-gather.2.cloned.1.call-update
  37.2 0.7 fusion.8
  38.0 0.1 broadcast_in_dim.5
  38.0 0.1 mul.38
  38.1 1.1 dynamic-slice_dynamic-update-slice_fusion.7
  39.2 1.1 dynamic-slice_dynamic-update-slice_fusion.6
  40.3 1.1 dynamic-slice_dynamic-update-slice_fusion.5
  41.4 0.0 copy-done
  41.4 0.2 dynamic-slice_dynamic-update-slice_fusion.4
  41.6 0.2 dynamic-slice_dynamic-update-slice_fusion.3
  41.8 0.2 dynamic-slice_dynamic-update-slice_fusion.2
  41.9 0.2 dynamic-slice_dynamic-update-slice_fusion.1
  42.1 0.2 dynamic-slice_dynamic-update-slice_fusion
  42.2 78.2 %all-gather.2.cloned.1.call-done = bf16[2048,2048]{1,0:T(8,128)(2,1)} async-done(((bf16[64,2048]{1,0:T(8,128)(2,1)}), bf16[2048,2048]{1,0:T(8,128)(2,1)}) %all-gather.2.cloned.1.call-update) | async-done | bytes 8388624 | tf_op jit(solution)/shard_map/all_gather | solution.py:63
  120.4 9.4 %convolution_multiply_fusion = f32[512,2048]{1,0:T(8,128)} fusion(bf16[512,2048]{1,0:T(8,128)(2,1)S(1)} %dynamic-slice_dynamic-update-slice_fusion, bf16[2048,2048]{1,0:T(8,128)(2,1)} %all-gather.2.cloned.1.call-done, f32[2048]{0:T(1024)S(1)} %mul.38), kind=kOutput, calls=%fused_computation | convolution fusion | flops 4296015872 | bytes 14688256 | tf_op jit(solution)/shard_map/dot_general | solution.py:74
  (3 shorter events, 0.1 us)
Async XLA Ops:
  6.5 113.9 %all-gather.2.cloned.1.call-start = ((), (), s32[]{:S(2)}) async-start(), calls=%async_computation.1 | async-start | bytes 8650752 | tf_op jit(solution)/shard_map/all_gather | solution.py:63
  6.5 9.3 %collective-permute-start = (f32[64,1024]{1,0:T(8,128)}, f32[64,1024]{1,0:T(8,128)S(1)}, u32[]{:S(2)}, u32[]{:S(2)}) collective-permute-start(f32[64,1024]{1,0:T(8,128)} %param.3), channel_id=1, source_target_pairs={{0,1},{1,2},{2,3},{3,4},{4,5},{5,6},{6,7},{7,8},{8,9},{9,10},{10,1... | collective-permute-start | bytes 786440 | tf_op jit(solution)/shard_map/ppermute | solution.py:16
  37.2 4.2 %copy-start = (bf16[64,2048]{1,0:T(8,128)(2,1)S(1)}, bf16[64,2048]{1,0:T(8,128)(2,1)}, u32[]{:S(2)}) copy-start(bf16[64,2048]{1,0:T(8,128)(2,1)} %fusion.2) | copy-start | bytes 786436
Sparse Core Ops, SparseCore 0:
  37.3 83.0 all-gather.1
